TPU v7x, 32 devices: a whole 2x2x4 slice. The times are simulated.
32 devices in a mesh: cand: 4 (over y, x), hist: 8 (over z, core).
Axes of the slice: x: 2, y: 2, z: 4, core: 2. Of those that a mesh axis runs over, the one named last changes fastest.
Arguments:
- cand_x: bfloat16 [2, 1024, 1024], P(None, ('cand', 'hist')), may hold values from -6 to 6
- qu_weight: bfloat16 [1024, 2048], replicated, may hold values from -0.1875 to 0.1875
- out_weight: bfloat16 [1024, 1024], replicated, may hold values from -0.1875 to 0.1875
- k_cache: bfloat16 [131072, 1024], P('hist', 'cand'), may hold values from -1.5 to 1.5
- v_cache: bfloat16 [131072, 1024], P('hist', 'cand'), may hold values from -6 to 6
- hist_len: int32 [16], replicated, may hold values from 1 to 32768, as said below
- cand_count: int32 [2, 16], replicated, may hold values from 1 to 128, 1024 in all within a row
- tile_user: int32 [1024], P('hist'), may hold values from 0 to 16, as said below
- tile_rank: int32 [1024], P('hist'), may hold values from 0 to 255, as said below
Outputs:
- ranked: bfloat16 [2, 1024, 1024], P(None, ('cand', 'hist'))
Inputs may be any that keep to these rules, and one draw needn't show every extreme that they name: A user's history fills exactly ceil(hist_len / 128) tile slots; one user's history is 32768 rows long. `tile_user`: slot owner, 16 for an empty slot; within each hist index's 128 slots the occupied ones come first; every user owns at least one slot. `tile_rank`: each tile position 0 to ceil(hist_len[u] / 128) - 1 of every user u stands in exactly one slot; empty slots hold 0. `cand_count`: row m gives the candidates of each user in micro-batch m, numbered user by user; they sum to 1024 and one user has exactly 128.
All inputs are finite; a program needn't handle non-finite values.
Results may differ from a plain program's by a relative error of at most 0.0051.
Values may be sent and summed in bfloat16 or wider, within the bound.
No kernel may reach another device: no remote copies, remote signals or barrier semaphores. Data moves between devices by JAX's collectives and lax.ppermute only.
A program may use at most 128 MiB of HBM per device.

v0:
```python
import jax
import jax.numpy as jnp
from jax import lax
from jax.sharding import PartitionSpec as P

HEAD_DIM = 128
TILE = 128
USERS = 16
MICRO = 2


EPSILON = 1e-06


def body(
    cand_x, qu_weight, out_weight, k_cache, v_cache, hist_len, cand_count, tile_user, tile_rank
):
    n_cand = lax.axis_size("cand")
    n_hist = lax.axis_size("hist")
    local_rows = cand_x.shape[1]
    model_width = cand_x.shape[2]
    head_cols = k_cache.shape[1]
    heads_here = head_cols // HEAD_DIM
    key_tiles = k_cache.reshape(-1, TILE, heads_here, HEAD_DIM)
    value_tiles = v_cache.reshape(-1, TILE, heads_here, HEAD_DIM)
    tiles_here = key_tiles.shape[0]
    per_turn = max(tiles_here // 8, 1)
    turn_count = tiles_here // per_turn
    user_ids = jnp.arange(USERS, dtype=jnp.int32)
    tile_rows = jnp.arange(TILE, dtype=jnp.int32)
    outputs = []
    for micro_index in range(MICRO):
        cand_rows = cand_x[micro_index]
        projected = jax.nn.silu(jnp.dot(cand_rows, qu_weight, preferred_element_type=jnp.float32))
        queries = projected[:, :model_width].astype(jnp.bfloat16)
        gate_vals = projected[:, model_width:].astype(jnp.bfloat16)
        gathered = lax.all_gather(queries, "hist", axis=0, tiled=True)
        queries_all = lax.all_to_all(gathered, "cand", split_axis=1, concat_axis=0, tiled=True)
        all_cands = queries_all.shape[0]
        window = 2 * all_cands // USERS
        counts = cand_count[micro_index]
        cand_start = jnp.cumsum(counts) - counts
        user_offsets = jnp.minimum(cand_start, all_cands - window)
        user_windows = jnp.stack(
            [
                lax.dynamic_slice_in_dim(queries_all, user_offsets[member], window, 0)
                for member in range(USERS)
            ]
        )
        row_ids = jnp.arange(window, dtype=jnp.int32)

        def visit_tiles(turn_index, user_sums):
            first_slot = turn_index * per_turn
            key_block = lax.dynamic_slice_in_dim(key_tiles, first_slot, per_turn, 0)
            value_block = lax.dynamic_slice_in_dim(value_tiles, first_slot, per_turn, 0)
            owners = lax.dynamic_slice_in_dim(tile_user, first_slot, per_turn, 0)
            positions = lax.dynamic_slice_in_dim(tile_rank, first_slot, per_turn, 0)
            matches = owners[:, None] == user_ids[None, :]
            length = jnp.sum(jnp.where(matches, hist_len[None, :], 0), axis=1)
            first_cand = jnp.sum(jnp.where(matches, cand_start[None, :], 0), axis=1)
            cand_total = jnp.sum(jnp.where(matches, counts[None, :], 0), axis=1)
            offsets = jnp.sum(jnp.where(matches, user_offsets[None, :], 0), axis=1)
            windows = jnp.einsum(
                "gu,uwc->gwc",
                matches.astype(jnp.bfloat16),
                user_windows,
                preferred_element_type=jnp.float32,
            ).astype(jnp.bfloat16)
            windows = windows.reshape(per_turn, window, heads_here, HEAD_DIM)
            scores = jnp.einsum(
                "gwhd,gkhd->ghwk", windows, key_block, preferred_element_type=jnp.float32
            )
            cand_ids = offsets[:, None] + row_ids[None, :]
            cand_ok = (cand_ids >= first_cand[:, None]) & (
                cand_ids < (first_cand + cand_total)[:, None]
            )
            key_ok = positions[:, None] * TILE + tile_rows[None, :] < length[:, None]
            keep_mask = cand_ok[:, None, :, None] & key_ok[:, None, None, :]
            weights = jnp.where(keep_mask, jax.nn.silu(scores), 0.0).astype(jnp.bfloat16)
            contrib = jnp.einsum(
                "ghwk,gkhd->gwhd", weights, value_block, preferred_element_type=jnp.float32
            )
            contrib = contrib.reshape(per_turn, window, head_cols)
            added = jnp.einsum(
                "gu,gwc->uwc", matches.astype(jnp.float32), contrib, precision=lax.Precision.HIGHEST
            )
            return user_sums + added

        user_sums = lax.fori_loop(
            0, turn_count, visit_tiles, jnp.zeros((USERS, window, head_cols), jnp.float32)
        )
        partial_value = jnp.zeros((all_cands, head_cols), jnp.float32)
        for member in range(USERS):
            current = lax.dynamic_slice_in_dim(partial_value, user_offsets[member], window, 0)
            partial_value = lax.dynamic_update_slice_in_dim(
                partial_value, current + user_sums[member], user_offsets[member], 0
            )
        blocks = partial_value.reshape(n_cand, n_hist, local_rows, head_cols)
        regrouped = lax.all_to_all(blocks, "cand", split_axis=0, concat_axis=3, tiled=True)
        attended = lax.psum_scatter(regrouped, "hist", scatter_dimension=1, tiled=True)
        attended = attended.reshape(local_rows, model_width)
        average = jnp.mean(attended, axis=-1, keepdims=True)
        centered = attended - average
        spread_sq = jnp.mean(centered * centered, axis=-1, keepdims=True)
        normed = centered * lax.rsqrt(spread_sq + EPSILON)
        mixed_rows = (normed * gate_vals.astype(jnp.float32)).astype(jnp.bfloat16)
        ranked = jnp.dot(
            mixed_rows, out_weight, preferred_element_type=jnp.float32
        ) + cand_rows.astype(jnp.float32)
        outputs.append(ranked.astype(jnp.bfloat16))
    return jnp.stack(outputs)


def solution(mesh):
    return jax.shard_map(
        body,
        mesh=mesh,
        in_specs=(
            P(None, ("cand", "hist"), None),
            P(),
            P(),
            P("hist", "cand"),
            P("hist", "cand"),
            P(),
            P(),
            P("hist"),
            P("hist"),
        ),
        out_specs=P(None, ("cand", "hist"), None),
        check_vma=False,
    )
```

profile of v0, /device:TPU:0, one launch (start us, length us, event | category | flops | bytes accessed | tf_op | source)
XLA Modules:
  0.0 605.9 jit_solution(5571507034580627950)
XLA Ops:
  6.5 3.2 multiply_convert_fusion.1
  9.8 16.7 %all_gather.6 = bf16[256,1024]{1,0:T(8,128)(2,1)S(1)} all-gather(bf16[32,1024]{1,0:T(8,128)(2,1)S(1)} %slice.354), channel_id=1, replica_groups=mesh['cand'=4,'hist'=8] {'hist'}, dimensions={0}, use_global_device_ids=true | all-gather | bytes 589824 | tf_op jit(solution)/shard_map/all_gather | solution.py:37
  27.4 3.7 all-to-all-start
  31.1 3.0 multiply_convert_fusion
  76.7 12.5 %reshape.390 = bf16[128,128,2,128]{3,2,1,0:T(2,128)(2,1)} reshape(bf16[16384,256]{1,0:T(8,128)(2,1)} %param.17) | data formatting | bytes 16777216 | tf_op jit(solution)/shard_map/reshape | solution.py:25
  89.3 20.7 %copy.112 = bf16[128,128,2,128]{1,3,2,0:T(8,128)(2,1)} copy(bf16[128,128,2,128]{3,2,1,0:T(2,128)(2,1)} %reshape.390) | data formatting | bytes 16777216
  110.0 12.5 %reshape.391 = bf16[128,128,2,128]{3,2,1,0:T(2,128)(2,1)} reshape(bf16[16384,256]{1,0:T(8,128)(2,1)} %param.16) | data formatting | bytes 16777216 | tf_op jit(solution)/shard_map/reshape | solution.py:24
  122.5 9.1 %copy.114 = bf16[128,128,2,128]{3,1,2,0:T(8,128)(2,1)} copy(bf16[128,128,2,128]{3,2,1,0:T(2,128)(2,1)} %reshape.391) | data formatting | bytes 16777216
  131.7 14.8 %all_gather.7 = bf16[256,1024]{1,0:T(8,128)(2,1)S(1)} all-gather(bf16[32,1024]{1,0:T(8,128)(2,1)S(1)} %slice.372), channel_id=1, replica_groups=mesh['cand'=4,'hist'=8] {'hist'}, dimensions={0}, use_global_device_ids=true | all-gather | bytes 589824 | tf_op jit(solution)/shard_map/all_gather | solution.py:37
  167.0 4.3 all-to-all-start.2
  173.6 129.4 %while.32 = (s32[]{:T(128)}, f32[16,128,256]{2,0,1:T(8,128)}, s32[128]{0:T(128)S(1)}, bf16[128,128,2,128]{1,3,2,0:T(8,128)(2,1)}, s32[16]{0:T(128)S(1)}, /*index...) while((s32[]{:T(128)}, f32[16,128,256]{2,0,1:T(8,128)}, ...), condition=%wide.region_6.7_spmd.clone.clone, body=%wide.region_1.6_spmd.clone.clone.sunk | while | flops 390871776 | bytes 20463428 | solution.py:89
  177.1 4.8 fusion.165
  181.9 3.1 copy.190
  185.1 4.1 select_add_fusion.4
  192.8 4.8 fusion.165
  197.6 3.1 copy.190
  200.7 4.7 select_add_fusion.4
  209.0 4.8 fusion.165
  213.8 3.1 copy.190
  217.0 4.7 select_add_fusion.4
  225.3 4.8 fusion.165
  230.1 3.1 copy.190
  233.2 4.7 select_add_fusion.4
  241.6 4.8 fusion.165
  246.3 3.1 copy.190
  249.5 4.7 select_add_fusion.4
  257.8 4.8 fusion.165
  262.6 3.1 copy.190
  265.7 4.7 select_add_fusion.4
  274.1 4.8 fusion.165
  278.8 3.1 copy.190
  282.0 4.7 select_add_fusion.4
  290.3 4.8 fusion.165
  295.1 3.1 copy.190
  298.3 4.7 select_add_fusion.4
  349.9 4.2 all-to-all-start.1
  370.6 130.0 %while.33 = (s32[]{:T(128)}, f32[16,128,256]{2,0,1:T(8,128)}, s32[128]{0:T(128)S(1)}, bf16[128,128,2,128]{1,3,2,0:T(8,128)(2,1)}, s32[16]{0:T(128)S(1)}, /*index...) while((s32[]{:T(128)}, f32[16,128,256]{2,0,1:T(8,128)}, ...), condition=%wide.region_16.17_spmd.clone.clone, body=%wide.region_11.16_spmd.clone.clone.sunk | while | flops 390871776 | bytes 20467012 | solution.py:89
  374.2 4.8 fusion.175
  379.0 3.1 copy.192
  382.1 4.1 select_add_fusion.5
  389.9 4.8 fusion.175
  394.7 3.1 copy.192
  397.8 4.8 select_add_fusion.5
  406.2 4.8 fusion.175
  411.0 3.1 copy.192
  414.2 4.8 select_add_fusion.5
  422.6 4.8 fusion.175
  427.3 3.1 copy.192
  430.5 4.8 select_add_fusion.5
  438.9 4.8 fusion.175
  443.7 3.1 copy.192
  446.8 4.8 select_add_fusion.5
  455.2 4.8 fusion.175
  460.0 3.1 copy.192
  463.2 4.8 select_add_fusion.5
  471.6 4.8 fusion.175
  476.3 3.1 copy.192
  479.5 4.8 select_add_fusion.5
  487.9 4.8 fusion.175
  492.7 3.1 copy.192
  495.8 4.8 select_add_fusion.5
  536.7 18.7 %all_to_all.74 = f32[4,8,32,256]{3,2,1,0:T(8,128)S(1)} all-to-all(f32[4,8,32,256]{3,2,1,0:T(8,128)S(1)} %bitcast.340), channel_id=1, replica_groups=mesh['cand'=4,'hist'=8] {'cand'}, dimensions={0} | all-to-all | bytes 2097152 | tf_op jit(solution)/shard_map/all_to_all | solution.py:99
  556.5 4.8 reduce-scatter.3.cloned.1.call-done
  563.5 30.7 %reduce-scatter.5.cloned.1.call-done = f32[1,1,32,1024]{3,2,1,0:T(8,128)} async-done(((f32[1,8,32,1024]{3,2,1,0:T(8,128)}), f32[1,1,32,1024]{3,2,1,0:T(8,128)}) %reduce-scatter.5.cloned.1.call-update) | async-done | bytes 131088 | tf_op jit(solution)/shard_map/reduce_scatter | solution.py:100
  (489 shorter events, 170.6 us)
Async XLA Ops:
  6.5 589.9 %copy-start = (bf16[1024,1024]{1,0:T(8,128)(2,1)S(1)}, bf16[1024,1024]{1,0:T(8,128)(2,1)}, u32[]{:S(2)}) copy-start(bf16[1024,1024]{1,0:T(8,128)(2,1)} %param.15) | copy-start | bytes 6291460
  9.8 17.6 %copy-start.5 = (bf16[32,2048]{1,0:T(8,128)(2,1)}, bf16[32,2048]{1,0:T(8,128)(2,1)S(1)}, u32[]{:S(2)}) copy-start(bf16[32,2048]{1,0:T(8,128)(2,1)S(1)} %multiply_convert_fusion.1) | copy-start | bytes 393220
  9.8 21.3 %copy-start.4 = (bf16[2,32,1024]{2,1,0:T(8,128)(2,1)S(1)}, bf16[2,32,1024]{2,1,0:T(8,128)(2,1)}, u32[]{:S(2)}) copy-start(bf16[2,32,1024]{2,1,0:T(8,128)(2,1)} %param.13) | copy-start | bytes 393220
  27.4 139.7 %all-to-all-start = ((bf16[256,4,256]{2,0,1:T(8,128)(2,1)}), bf16[256,4,256]{2,0,1:T(8,128)(2,1)S(1)}, u32[]{:S(2)}, u32[]{:S(2)}) async-start(bf16[256,4,256]{2,0,1:T(8,128)(2,1)} %bitcast.313), calls=%async_computation | async-start | bytes 1048576 | tf_op jit(solution)/shard_map/all_to_all | solution.py:38
  34.2 97.5 %copy-start.7 = (bf16[32,2048]{1,0:T(8,128)(2,1)}, bf16[32,2048]{1,0:T(8,128)(2,1)S(1)}, u32[]{:S(2)}) copy-start(bf16[32,2048]{1,0:T(8,128)(2,1)S(1)} %multiply_convert_fusion) | copy-start | bytes 393220
  167.0 182.9 %all-to-all-start.2 = ((bf16[256,4,256]{2,0,1:T(8,128)(2,1)}), bf16[256,4,256]{2,0,1:T(8,128)(2,1)}, u32[]{:S(2)}, u32[]{:S(2)}) async-start(bf16[256,4,256]{2,0,1:T(8,128)(2,1)} %bitcast.312), calls=%async_computation.3 | async-start | bytes 1048576 | tf_op jit(solution)/shard_map/all_to_all | solution.py:38
  200.7 4.7 copy-start.17
  200.7 4.7 copy-start.20
  200.7 4.7 copy-start.24
  217.0 4.7 copy-start.17
  217.0 4.7 copy-start.20
  217.0 4.7 copy-start.24
  233.2 4.7 copy-start.17
  233.2 4.7 copy-start.20
  233.2 4.7 copy-start.24
  249.5 4.7 copy-start.13
  249.5 4.7 copy-start.17
  249.5 4.7 copy-start.20
  249.5 4.7 copy-start.24
  265.7 4.7 copy-start.13
  265.7 4.7 copy-start.17
  265.7 4.7 copy-start.20
  265.7 4.7 copy-start.24
  282.0 4.7 copy-start.17
  282.0 4.7 copy-start.20
  282.0 4.7 copy-start.24
  298.2 4.7 copy-start.17
  298.3 4.7 copy-start.20
  298.3 4.7 copy-start.24
  349.9 174.8 %all-to-all-start.1 = ((f32[4,8,32,256]{3,2,1,0:T(8,128)}), f32[4,8,32,256]{3,2,1,0:T(8,128)}, u32[]{:S(2)}, u32[]{:S(2)}) async-start(f32[4,8,32,256]{3,2,1,0:T(8,128)} %bitcast.54), calls=%async_computation.1 | async-start | bytes 2097152 | tf_op jit(solution)/shard_map/all_to_all | solution.py:99
  354.2 207.2 %reduce-scatter.3.cloned.1.call-start = ((), (), s32[]{:S(2)}) async-start(), calls=%async_computation.6 | async-start | bytes 1179648 | tf_op jit(solution)/shard_map/reduce_scatter | solution.py:100
  354.4 16.2 %copy-start.10 = (s32[1,16]{1,0:T(1,128)S(1)}, s32[1,16]{1,0:T(1,128)}, u32[]{:S(2)}) copy-start(s32[1,16]{1,0:T(1,128)} %get-tuple-element.955) | copy-start | bytes 196
  354.5 16.2 %copy-start.14 = (s32[16]{0:T(128)S(1)}, s32[16]{0:T(128)}, u32[]{:S(2)}) copy-start(s32[16]{0:T(128)} %get-tuple-element.954) | copy-start | bytes 196
  397.8 4.8 copy-start.11
  397.8 4.8 copy-start.15
  397.8 4.8 copy-start.22
  397.8 4.8 copy-start.26
  414.1 4.8 copy-start.11
  414.1 4.8 copy-start.15
  414.1 4.8 copy-start.22
  414.1 4.8 copy-start.26
  430.5 4.8 copy-start.11
  430.5 4.8 copy-start.15
  430.5 4.8 copy-start.22
  430.5 4.8 copy-start.26
  446.8 4.8 copy-start.11
  446.8 4.8 copy-start.15
  446.8 4.8 copy-start.22
  446.8 4.8 copy-start.26
  463.1 4.8 copy-start.11
  463.2 4.8 copy-start.15
  463.2 4.8 copy-start.22
  463.2 4.8 copy-start.26
  479.5 4.8 copy-start.11
  479.5 4.8 copy-start.15
  479.5 4.8 copy-start.22
  479.5 4.8 copy-start.26
  495.8 4.8 copy-start.11
  495.8 4.8 copy-start.15
  495.8 4.8 copy-start.22
  495.8 4.8 copy-start.26
  527.1 67.1 %reduce-scatter.5.cloned.1.call-start = ((), (), s32[]{:S(2)}) async-start(), calls=%async_computation.7 | async-start | bytes 1179648 | tf_op jit(solution)/shard_map/reduce_scatter | solution.py:100
  555.4 41.1 %copy-start.6 = (bf16[32,2048]{1,0:T(8,128)(2,1)S(1)}, bf16[32,2048]{1,0:T(8,128)(2,1)}, u32[]{:S(2)}) copy-start(bf16[32,2048]{1,0:T(8,128)(2,1)} %copy-done.5) | copy-start | bytes 393220
  556.5 41.4 %copy-start.8 = (bf16[32,2048]{1,0:T(8,128)(2,1)S(1)}, bf16[32,2048]{1,0:T(8,128)(2,1)}, u32[]{:S(2)}) copy-start(bf16[32,2048]{1,0:T(8,128)(2,1)} %copy-done.7) | copy-start | bytes 393220
  (52 other events, 95.6 us)
Sparse Core Ops, SparseCore 0:
  527.2 34.0 reduce-scatter.2
  563.6 30.5 reduce-scatter.4
where the time goes:
time: 612 us; the launch traced here: 606 us
  local copies, waits for them, and re-layouts  203 us (33%)
  matrix products  186 us (30%)
  between operations  73.4 us (12%)
  blocking collectives  50.2 us (8%)
  other arithmetic  43.3 us (7%)
  waiting for transfers between devices  35.6 us (6%)
  starting transfers between devices  12.6 us (2%)
    dot_general x16, matrix products, visit_tiles(): jnp.einsum('ghwk,gkhd->gwhd', weights, value_block, preferred_element_typ...  76.4 us
    dot_general x16, matrix products, visit_tiles(): jnp.einsum('gu,gwc->uwc', matches.astype(jnp.float32), contrib, precision...  74.5 us
    reshape x16, local copies, waits for them, and re-layouts, visit_tiles(): contrib = contrib.reshape(per_turn, window, head_cols)  50.3 us
    unnamed x64, local copies, waits for them, and re-layouts  49.8 us
    dynamic_update_slice x32, local copies, waits for them, and re-layouts, body(): lax.dynamic_update_slice_in_dim(partial_value, current + user_sums[member...  41.6 us
    reduce_scatter x2, waiting for transfers between devices, body(): lax.psum_scatter(regrouped, 'hist', scatter_dimension=1, tiled=True)  35.6 us
    all_gather x2, blocking collectives, body(): gathered = lax.all_gather(queries, 'hist', axis=0, tiled=True)  31.5 us
    add x30, other arithmetic, body(): current + user_sums[member]  27.9 us
  transfers between devices with their start and end apart: 5, of which 2 were waited for; matrix products, arithmetic and copies ran while one was open for 69% of the time, Pallas kernels for 0%

commit v1 on v0

v1 whole, which is shorter than its diff:
```python
import functools

import jax
import jax.numpy as jnp
from jax import lax
from jax.experimental import pallas as pl
from jax.experimental.pallas import tpu as pltpu
from jax.sharding import PartitionSpec as P

HEAD_DIM = 128
TILE = 128
USERS = 16
MICRO = 2
BLOCK_TILES = 8
FIELDS = 2 + 4 * MICRO


EPSILON = 1e-06


def attend_kernel(info_ref, last_ref, q_ref, k_ref, v_ref, out_ref, *, window, heads_here):
    block = pl.program_id(0)

    @pl.when(block == 0)
    def _():
        out_ref[...] = jnp.zeros_like(out_ref)

    row_ids = lax.broadcasted_iota(jnp.int32, (window, 1), 0)
    key_ids = lax.broadcasted_iota(jnp.int32, (TILE, 1), 0)

    def one_tile(j, carry):
        base = (block * BLOCK_TILES + j) * FIELDS

        @pl.when(info_ref[base] > 0)
        def _():
            klen = info_ref[base + 1]
            rows = pl.ds(pl.multiple_of(j * TILE, TILE), TILE)
            keys = jnp.where(key_ids < klen, k_ref[rows, :], 0)
            values = v_ref[rows, :]
            for m in range(MICRO):
                base_row = pl.multiple_of(info_ref[base + 2 + 4 * m], 8)
                shift = info_ref[base + 3 + 4 * m]
                lo = info_ref[base + 4 + 4 * m]
                hi = info_ref[base + 5 + 4 * m]
                span = pl.ds(base_row, window + 8)
                padded_q = q_ref[m, span, :]
                window_q = pltpu.roll(padded_q, (window + 8 - shift) % (window + 8), 0)[:window]
                keep = (row_ids >= lo) & (row_ids < hi)
                window_q = jnp.where(keep, window_q, 0.0).astype(jnp.bfloat16)
                parts = []
                for h in range(heads_here):
                    cols = slice(h * HEAD_DIM, (h + 1) * HEAD_DIM)
                    scores = lax.dot_general(
                        window_q[:, cols],
                        keys[:, cols],
                        (((1,), (1,)), ((), ())),
                        preferred_element_type=jnp.float32,
                    )
                    weights = (scores / (1.0 + jnp.exp(-scores))).astype(jnp.bfloat16)
                    parts.append(
                        jnp.dot(weights, values[:, cols], preferred_element_type=jnp.float32)
                    )
                contrib = parts[0] if heads_here == 1 else jnp.concatenate(parts, axis=1)
                contrib = jnp.concatenate([contrib, jnp.zeros((8, contrib.shape[1]), contrib.dtype)])
                out_ref[m, span, :] += pltpu.roll(contrib, shift, 0)

        return carry

    lax.fori_loop(0, BLOCK_TILES, one_tile, 0)


def body(
    cand_x, qu_weight, out_weight, k_cache, v_cache, hist_len, cand_count, tile_user, tile_rank
):
    n_cand = lax.axis_size("cand")
    n_hist = lax.axis_size("hist")
    micro, local_rows, model_width = cand_x.shape
    head_cols = k_cache.shape[1]
    heads_here = head_cols // HEAD_DIM
    tiles_here = k_cache.shape[0] // TILE

    cand_rows = cand_x.reshape(micro * local_rows, model_width)
    projected = jax.nn.silu(jnp.dot(cand_rows, qu_weight, preferred_element_type=jnp.float32))
    queries = projected[:, :model_width].astype(jnp.bfloat16).reshape(micro, local_rows, model_width)
    gate_vals = projected[:, model_width:].astype(jnp.bfloat16)
    gathered = lax.all_gather(queries, "hist", axis=1, tiled=True)
    queries_all = lax.all_to_all(gathered, "cand", split_axis=2, concat_axis=1, tiled=True)
    all_cands = queries_all.shape[1]
    window = 2 * all_cands // USERS

    starts = jnp.cumsum(cand_count, axis=1) - cand_count
    offsets = jnp.minimum(starts, all_cands - window)
    base_rows = jnp.minimum(offsets // 8 * 8, all_cands - window - 8)
    shifts = offsets - base_rows
    lows = starts - offsets
    highs = lows + cand_count
    occupied = tile_user < USERS
    owner = jnp.minimum(tile_user, USERS - 1)
    key_len = hist_len[owner] - tile_rank * TILE
    fields = [occupied.astype(jnp.int32), key_len]
    for m in range(micro):
        fields += [base_rows[m][owner], shifts[m][owner], lows[m][owner], highs[m][owner]]
    info = jnp.stack(fields, axis=1).astype(jnp.int32).reshape(-1)
    block_ids = jnp.arange(tiles_here, dtype=jnp.int32) // BLOCK_TILES
    last_block = jnp.max(jnp.where(occupied, block_ids, 0)).reshape(1).astype(jnp.int32)

    rows_per_block = BLOCK_TILES * TILE
    n_blocks = tiles_here // BLOCK_TILES
    whole = pl.BlockSpec((micro, all_cands, head_cols), lambda b, info, last: (0, 0, 0))
    tiles = pl.BlockSpec(
        (rows_per_block, head_cols), lambda b, info, last: (jnp.minimum(b, last[0]), 0)
    )
    partial_value = pl.pallas_call(
        functools.partial(attend_kernel, window=window, heads_here=heads_here),
        grid_spec=pltpu.PrefetchScalarGridSpec(
            num_scalar_prefetch=2,
            grid=(n_blocks,),
            in_specs=[whole, tiles, tiles],
            out_specs=whole,
        ),
        out_shape=jax.ShapeDtypeStruct((micro, all_cands, head_cols), jnp.float32),
        compiler_params=pltpu.CompilerParams(dimension_semantics=("arbitrary",)),
    )(info, last_block, queries_all.astype(jnp.float32), k_cache, v_cache)

    blocks = partial_value.reshape(micro, n_cand, n_hist, local_rows, head_cols)
    reduced = lax.psum_scatter(blocks, "hist", scatter_dimension=2, tiled=True)
    reduced = reduced.reshape(micro, n_cand, local_rows, head_cols)
    attended = lax.all_to_all(reduced, "cand", split_axis=1, concat_axis=3, tiled=True)
    attended = attended.reshape(micro * local_rows, model_width)
    average = jnp.mean(attended, axis=-1, keepdims=True)
    centered = attended - average
    spread_sq = jnp.mean(centered * centered, axis=-1, keepdims=True)
    normed = centered * lax.rsqrt(spread_sq + EPSILON)
    mixed_rows = (normed * gate_vals.astype(jnp.float32)).astype(jnp.bfloat16)
    ranked = jnp.dot(
        mixed_rows, out_weight, preferred_element_type=jnp.float32
    ) + cand_rows.astype(jnp.float32)
    return ranked.astype(jnp.bfloat16).reshape(micro, local_rows, model_width)


def solution(mesh):
    return jax.shard_map(
        body,
        mesh=mesh,
        in_specs=(
            P(None, ("cand", "hist"), None),
            P(),
            P(),
            P("hist", "cand"),
            P("hist", "cand"),
            P(),
            P(),
            P("hist"),
            P("hist"),
        ),
        out_specs=P(None, ("cand", "hist"), None),
        check_vma=False,
    )
```

time: 612 us -> 313 us (0.51); the launches traced: 606 us -> 315 us
  local copies, waits for them, and re-layouts: 203 us -> 19.4 us
  matrix products: 186 us -> 4.47 us
  waiting for transfers between devices: 35.6 us -> 114 us
  between operations: 73.4 us -> 13.6 us
  Pallas kernels: 0 us -> 57.6 us
  other arithmetic: 43.3 us -> 92.2 us
  blocking collectives: 50.2 us -> 9.17 us
  starting transfers between devices: 12.6 us -> 5.17 us
    dot_general x48 -> x0, matrix products: 178 us -> none  [the longest x16 76.4 us: visit_tiles(): jnp.einsum('ghwk,gkhd->gwhd', weights, value_block, preferred_element_typ...]
    unnamed x2 -> x3, waiting for transfers between devices: 0.03 us -> 114 us
    reshape x34 -> x4, local copies, waits for them, and re-layouts: 93.6 us -> 3.16 us  [the longest x2 1.64 us: body(): reduced = reduced.reshape(micro, n_cand, local_rows, head_cols)]
    another operation x5 -> x10, other arithmetic: 0.98 us -> 79.7 us  [the longest x9 79.5 us: body(): info = jnp.stack(fields, axis=1).astype(jnp.int32).reshape(-1)]
    pallas_call x0 -> x1, Pallas kernels: none -> 57.6 us  [body(): pl.pallas_call(functools.partial(attend_kernel, window=window, heads_here...]
    unnamed x64 -> x16, local copies, waits for them, and re-layouts: 49.8 us -> 1.28 us
    dynamic_update_slice x32 -> x0, local copies, waits for them, and re-layouts: 41.6 us -> none  [body(): lax.dynamic_update_slice_in_dim(partial_value, current + user_sums[member...]
    reduce_scatter x2 -> x0, waiting for transfers between devices: 35.6 us -> none  [body(): lax.psum_scatter(regrouped, 'hist', scatter_dimension=1, tiled=True)]
  transfers between devices with their start and end apart: 5 -> 3, of which waited for: 2 -> 1; matrix products, arithmetic and copies ran while one was open for 69% -> 31% of each run, Pallas kernels for 0% -> 0%
where the time goes in v1:
time: 313 us; the launch traced here: 315 us
  waiting for transfers between devices  114 us (36%)
  other arithmetic  92.2 us (29%)
  Pallas kernels  57.6 us (18%)
  local copies, waits for them, and re-layouts  19.4 us (6%)
  between operations  13.6 us (4%)
  blocking collectives  9.17 us (3%)
  starting transfers between devices  5.17 us (2%)
  matrix products  4.47 us (1%)
    unnamed x3, waiting for transfers between devices  114 us
    another operation x9, other arithmetic, body(): info = jnp.stack(fields, axis=1).astype(jnp.int32).reshape(-1)  79.5 us
    pallas_call x1, Pallas kernels, body(): pl.pallas_call(functools.partial(attend_kernel, window=window, heads_here...  57.6 us
    reduce_max x1, other arithmetic, body(): jnp.max(jnp.where(occupied, block_ids, 0)).reshape(1).astype(jnp.int32)  10.7 us
    all_to_all x1, blocking collectives, body(): lax.all_to_all(reduced, 'cand', split_axis=1, concat_axis=3, tiled=True)  9.17 us
  transfers between devices with their start and end apart: 3, of which 1 were waited for; matrix products, arithmetic and copies ran while one was open for 31% of the time, Pallas kernels for 0%

profile of v1, /device:TPU:0, one launch (start us, length us, event | category | flops | bytes accessed | tf_op | source)
XLA Modules:
  0.0 315.2 jit_solution(18212490672145247582)
XLA Ops:
  6.5 0.0 copy-start
  6.5 0.0 all-gather.2.cloned.1.call-start
  6.5 0.0 copy-start.4
  6.5 0.0 copy-start.3
  6.5 3.3 %multiply_convert_fusion = bf16[64,2048]{1,0:T(8,128)(2,1)S(1)} fusion(bf16[64,1024]{1,0:T(8,128)(2,1)} %bitcast.202, bf16[1024,2048]{1,0:T(8,128)(2,1)} %param.10), kind=kOutput, calls=%fused_computation.3 | convolution fusion | flops 269090816 | bytes 4587520 | tf_op jit(solution)/shard_map/dot_general | solution.py:83
  9.8 0.8 copy.16
  10.6 0.0 all-gather.2.cloned.1.call-update
  10.7 0.0 copy-done.4
  10.7 0.2 reduce_window_sum.11
  10.9 0.7 fusion.12
  11.6 0.7 fusion.13
  12.3 0.7 fusion.9
  13.0 0.7 fusion.11
  13.7 0.7 fusion.15
  14.4 0.7 fusion.8
  15.1 0.7 fusion.10
  15.9 0.7 fusion.14
  16.6 0.0 copy-done.3
  16.6 10.7 %fusion.5 = (s32[]{:T(128)}, s32[128,1]{0,1:T(1,128)S(1)}) fusion(s32[128]{0:T(128)S(1)} %copy-done.3, s32[]{:T(128)} %bitcast.118, s32[]{:T(128)} %bitcast.117, s32[]{:T(128)} %bitcast.116, s32[]{:T(128)} %bitcast.115, s32[]{:T(128)} %bitcast.114, s32[]{:T(128)} %bitcast.113, s32[]{:T(128)} %bitcast.112, s32[]{:T(128)} %bitcast.111, s32[]{:T(128)} %bitcast.110, ...), kind=kLoop, calls=%fused_computation.26 | loop fusion | flops 5759 | bytes 1092 | tf_op jit(solution)/shard_map/reduce_max | solution.py:105
  27.3 9.8 %select_bitcast_fusion = s32[128,1]{0,1:T(1,128)S(1)} fusion(s32[]{:T(128)} %bitcast.137, s32[]{:T(128)} %bitcast.138, s32[]{:T(128)} %bitcast.139, s32[]{:T(128)} %bitcast.140, s32[]{:T(128)} %bitcast.141, s32[]{:T(128)} %bitcast.142, s32[]{:T(128)} %bitcast.143, s32[]{:T(128)} %bitcast.144, s32[]{:T(128)} %bitcast.145, s32[]{:T(128)} %bitcast.146, ...), kind=kLoop, calls=%fused_computation.27 | loop fusion | flops 4352 | bytes 1088 | tf_op jit(solution)/shard_map/stack | solution.py:103
  37.1 9.8 %select_bitcast_fusion.1 = s32[128,1]{0,1:T(1,128)S(1)} fusion(s32[]{:T(128)} %bitcast.120, s32[]{:T(128)} %bitcast.121, s32[]{:T(128)} %bitcast.122, s32[]{:T(128)} %bitcast.123, s32[]{:T(128)} %bitcast.124, s32[]{:T(128)} %bitcast.125, s32[]{:T(128)} %bitcast.126, s32[]{:T(128)} %bitcast.127, s32[]{:T(128)} %bitcast.128, s32[]{:T(128)} %bitcast.129, ...), kind=kLoop, calls=%fused_computation.28 | loop fusion | flops 4352 | bytes 1088 | tf_op jit(solution)/shard_map/stack | solution.py:103
  46.9 9.9 %select_bitcast_fusion.3 = s32[128,1]{0,1:T(1,128)S(1)} fusion(s32[]{:T(128)} %bitcast.86, s32[]{:T(128)} %bitcast.87, s32[]{:T(128)} %bitcast.88, s32[]{:T(128)} %bitcast.89, s32[]{:T(128)} %bitcast.90, s32[]{:T(128)} %bitcast.91, s32[]{:T(128)} %bitcast.92, s32[]{:T(128)} %bitcast.93, s32[]{:T(128)} %bitcast.94, s32[]{:T(128)} %bitcast.95, s32[]{:T(128)} %bitcast.96, ...), kind=kLoop, calls=%fused_computation.30 | loop fusion | flops 4352 | bytes 1088 | tf_op jit(solution)/shard_map/stack | solution.py:103
  56.9 9.9 %select_bitcast_fusion.5 = s32[128,1]{0,1:T(1,128)S(1)} fusion(s32[]{:T(128)} %bitcast.52, s32[]{:T(128)} %bitcast.53, s32[]{:T(128)} %bitcast.54, s32[]{:T(128)} %bitcast.55, s32[]{:T(128)} %bitcast.56, s32[]{:T(128)} %bitcast.57, s32[]{:T(128)} %bitcast.58, s32[]{:T(128)} %bitcast.59, s32[]{:T(128)} %bitcast.60, s32[]{:T(128)} %bitcast.61, s32[]{:T(128)} %bitcast.62, ...), kind=kLoop, calls=%fused_computation.32 | loop fusion | flops 4352 | bytes 1088 | tf_op jit(solution)/shard_map/stack | solution.py:103
  66.8 9.9 %select_bitcast_fusion.7 = s32[128,1]{0,1:T(1,128)S(1)} fusion(s32[]{:T(128)} %bitcast.18, s32[]{:T(128)} %bitcast.19, s32[]{:T(128)} %bitcast.20, s32[]{:T(128)} %bitcast.21, s32[]{:T(128)} %bitcast.22, s32[]{:T(128)} %bitcast.23, s32[]{:T(128)} %bitcast.24, s32[]{:T(128)} %bitcast.25, s32[]{:T(128)} %bitcast.26, s32[]{:T(128)} %bitcast.27, s32[]{:T(128)} %bitcast.28, ...), kind=kLoop, calls=%fused_computation.34 | loop fusion | flops 4352 | bytes 1088 | tf_op jit(solution)/shard_map/stack | solution.py:103
  76.7 0.0 copy-start.2
  76.7 0.0 copy-start.5
  76.7 0.0 all-gather.2.cloned.1.call-done
  76.8 4.9 %copy.17 = bf16[2,256,1024]{1,0,2:T(2,128)(2,1)} copy(bf16[2,256,1024]{2,0,1:T(2,128)(2,1)} %all-gather.2.cloned.1.call-done) | data formatting | bytes 2097152 | tf_op jit(solution)/shard_map/all_gather | solution.py:86
  81.7 5.2 %all-to-all-start = ((bf16[2,256,1024]{1,0,2:T(2,128)(2,1)}), bf16[2,256,1024]{1,0,2:T(2,128)(2,1)S(1)}, u32[]{:S(2)}, u32[]{:S(2)}) async-start(bf16[2,256,1024]{1,0,2:T(2,128)(2,1)} %copy.17), calls=%async_computation | async-start | bytes 2097152 | tf_op jit(solution)/shard_map/all_to_all | solution.py:87
  86.9 0.0 all-reduce.3.cloned.1.call-start
  86.9 0.0 copy-done.2
  86.9 0.7 fusion.16
  87.6 10.2 %select_bitcast_fusion.4 = s32[128,1]{0,1:T(1,128)S(1)} fusion(s32[]{:T(128)} %bitcast.69, s32[]{:T(128)} %bitcast.70, s32[]{:T(128)} %bitcast.71, s32[]{:T(128)} %bitcast.72, s32[]{:T(128)} %bitcast.73, s32[]{:T(128)} %bitcast.74, s32[]{:T(128)} %bitcast.75, s32[]{:T(128)} %bitcast.76, s32[]{:T(128)} %bitcast.77, s32[]{:T(128)} %bitcast.78, s32[]{:T(128)} %bitcast.79, ...), kind=kLoop, calls=%fused_computation.31 | loop fusion | flops 4352 | bytes 1088 | tf_op jit(solution)/shard_map/stack | solution.py:103
  97.8 9.9 %select_bitcast_fusion.6 = s32[128,1]{0,1:T(1,128)S(1)} fusion(s32[]{:T(128)} %bitcast.35, s32[]{:T(128)} %bitcast.36, s32[]{:T(128)} %bitcast.37, s32[]{:T(128)} %bitcast.38, s32[]{:T(128)} %bitcast.39, s32[]{:T(128)} %bitcast.40, s32[]{:T(128)} %bitcast.41, s32[]{:T(128)} %bitcast.42, s32[]{:T(128)} %bitcast.43, s32[]{:T(128)} %bitcast.44, s32[]{:T(128)} %bitcast.45, ...), kind=kLoop, calls=%fused_computation.33 | loop fusion | flops 4352 | bytes 1088 | tf_op jit(solution)/shard_map/stack | solution.py:103
  107.7 0.0 copy-done.5
  107.7 10.0 %fusion.6 = s32[128,1]{0,1:T(1,128)S(1)} fusion(s32[128]{0:T(128)S(1)} %copy-done.5, s32[]{:T(128)} %bitcast.1, s32[]{:T(128)} %bitcast.2, s32[]{:T(128)} %bitcast.3, s32[]{:T(128)} %bitcast.4, s32[]{:T(128)} %bitcast.5, s32[]{:T(128)} %bitcast.6, s32[]{:T(128)} %bitcast.7, s32[]{:T(128)} %bitcast.8, s32[]{:T(128)} %bitcast.9, s32[]{:T(128)} %bitcast.10, ...), kind=kLoop, calls=%fused_computation.36 | loop fusion | flops 4608 | bytes 1600 | tf_op jit(solution)/shard_map/stack | solution.py:103
  117.8 0.1 copy.15
  117.9 0.7 reshape.69.info_ref
  118.7 0.0 all-to-all-done
  118.7 0.1 copy.18
  118.8 1.5 convert_bitcast_fusion
  120.3 2.9 copy.19
  123.2 57.6 %shard_map.91 = f32[2,1024,256]{2,1,0:T(8,128)} custom-call(s32[1280]{0:T(1024)} %reshape.69.info_ref, s32[1]{0:T(128)} %bitcast.154.last_ref, f32[2,1024,256]{2,1,0:T(8,128)} %bitcast.196, bf16[16384,256]{1,0:T(8,128)(2,1)} %k_ref.1, bf16[16384,256]{1,0:T(8,128)(2,1)} %v_ref.1), custom_call_target="tpu_custom_call" | custom-call | tf_op jit(solution)/shard_map/pallas_call | solution.py:113
  180.9 0.0 copy-start.6
  180.9 0.0 all-reduce.3.cloned.1.call-update
  180.9 0.0 copy-start.1
  180.9 0.6 copy-done.6
  181.5 0.6 dynamic-slice
  182.1 113.5 %all-reduce.3.cloned.1.call-done = f32[2,4,8,32,256]{4,3,2,1,0:T(8,128)} async-done(((f32[2,4,8,32,256]{4,3,2,1,0:T(8,128)}), f32[2,4,8,32,256]{4,3,2,1,0:T(8,128)}) %all-reduce.3.cloned.1.call-update) | async-done | bytes 2097168
  295.6 1.6 dynamic-slice_bitcast_fusion
  297.3 9.2 %all_to_all.24 = f32[2,4,32,256]{3,2,0,1:T(8,128)S(1)} all-to-all(f32[2,4,32,256]{3,2,0,1:T(8,128)S(1)} %copy.20), channel_id=1, replica_groups=mesh['cand'=4,'hist'=8] {'cand'}, dimensions={1} | all-to-all | bytes 524288 | tf_op jit(solution)/shard_map/all_to_all | solution.py:128
  306.4 0.1 bitcast_reduce_fusion
  306.6 0.1 div.40
  306.6 0.2 multiply_reduce_fusion
  306.8 0.1 rsqrt.12
  306.9 0.2 copy.21
  307.1 0.0 copy-done
  307.2 0.0 copy-done.1
  307.2 1.2 fusion
  (8 shorter events, 0.2 us)
Async XLA Ops:
  6.5 300.6 %copy-start = (bf16[1024,1024]{1,0:T(8,128)(2,1)S(1)}, bf16[1024,1024]{1,0:T(8,128)(2,1)}, u32[]{:S(2)}) copy-start(bf16[1024,1024]{1,0:T(8,128)(2,1)} %param.11) | copy-start | bytes 6291460
  6.5 70.2 %all-gather.2.cloned.1.call-start = ((), (), s32[]{:S(2)}) async-start(), calls=%async_computation.2 | async-start | bytes 1179648 | tf_op jit(solution)/shard_map/all_gather | solution.py:86
  6.5 4.1 %copy-start.4 = (s32[2,16]{1,0:T(2,128)S(1)}, s32[2,16]{1,0:T(2,128)}, u32[]{:S(2)}) copy-start(s32[2,16]{1,0:T(2,128)} %param.15) | copy-start | bytes 388
  6.5 10.0 %copy-start.3 = (s32[128]{0:T(128)S(1)}, s32[128]{0:T(128)}, u32[]{:S(2)}) copy-start(s32[128]{0:T(128)} %param.16) | copy-start | bytes 1540
  76.7 10.1 %copy-start.2 = (s32[16]{0:T(128)S(1)}, s32[16]{0:T(128)}, u32[]{:S(2)}) copy-start(s32[16]{0:T(128)} %param.14) | copy-start | bytes 196
  76.7 31.0 %copy-start.5 = (s32[128]{0:T(128)S(1)}, s32[128]{0:T(128)}, u32[]{:S(2)}) copy-start(s32[128]{0:T(128)} %param.17) | copy-start | bytes 1540
  81.7 37.0 %all-to-all-start = ((bf16[2,256,1024]{1,0,2:T(2,128)(2,1)}), bf16[2,256,1024]{1,0,2:T(2,128)(2,1)S(1)}, u32[]{:S(2)}, u32[]{:S(2)}) async-start(bf16[2,256,1024]{1,0,2:T(2,128)(2,1)} %copy.17), calls=%async_computation | async-start | bytes 2097152 | tf_op jit(solution)/shard_map/all_to_all | solution.py:87
  86.9 208.8 %all-reduce.3.cloned.1.call-start = ((), (), s32[]{:S(2)}) async-start(), calls=%async_computation.3 | async-start | bytes 4194304
  180.9 0.7 copy-start.6
  180.9 126.3 %copy-start.1 = (bf16[2,32,1024]{2,1,0:T(8,128)(2,1)S(1)}, bf16[2,32,1024]{2,1,0:T(8,128)(2,1)}, u32[]{:S(2)}) copy-start(bf16[2,32,1024]{2,1,0:T(8,128)(2,1)} %param.9) | copy-start | bytes 393220
Sparse Core Ops, SparseCore 0:
  10.8 24.7 all-gather.1
  181.0 114.5 all-reduce.2
